TPU v7x, 32 devices: a whole 2x2x4 slice. The times are simulated.
32 devices in a mesh: exp: 4 (over z), row: 4 (over y, core), col: 2 (over x).
Axes of the slice: x: 2, y: 2, z: 4, core: 2. Of those that a mesh axis runs over, the one named last changes fastest.
Arguments:
- exposures: float32 [64, 128, 1024], P('exp', 'row', 'col'), may hold values from -6 to 6
- bad_pixels: int32 [64, 128, 1024], P('exp', 'row', 'col'), may hold values 0 or 1
- offsets: int32 [64, 2], P('exp'), may hold values from -8 to 8, as said below
- warp_index: int32 [64, 2], P('exp'), may hold values from 0 to 15
- blur_index: int32 [64], P('exp'), may hold values from 0 to 7
Outputs:
- residual: float32 [64, 128, 1024], P('exp', 'row', 'col')
- median_sky: float32 [128, 1024], P('row', 'col')
Inputs may be any that keep to these rules, and one draw needn't show every extreme that they name: `offsets`: in each component some exposure has the offset -8 and some has 8.
All inputs are finite; a program needn't handle non-finite values. No bound on the sum of `bad_pixels` on one device may be relied on, other than what follows from the above.
Results may differ from a plain program's by a relative error of at most 0.0003.
Values sent between devices are 32-bit elements; how exact they have to be, the bound alone decides.
No kernel may reach another device: no remote copies, remote signals or barrier semaphores. Data moves between devices by JAX's collectives and lax.ppermute only.
A program may use at most 64 MiB of HBM per device.

v0:
```python
import jax
import jax.numpy as jnp
from jax import lax
from jax.sharding import PartitionSpec as P

NFRAC = 16
NPSF = 8
PSF_RADIUS = 4
PASSES = 16
HALO = 11
sentinel = 1000000.0
half_sentinel = 500000.0
pivot_span = 16.0


def _grid_pairs(nrow, ncol, dr, dc, flat):
    pairs = []
    for r in range(nrow):
        for c in range(ncol):
            tr, tc = (r - dr, c - dc)
            if 0 <= tr < nrow and 0 <= tc < ncol:
                pairs.append((flat(r, c), flat(tr, tc)))
    return pairs


def extended(block, row_dim, col_dim, width):
    nrow = lax.axis_size("row")
    ncol = lax.axis_size("col")
    rows = block.shape[row_dim]
    cols = block.shape[col_dim]

    def piece(dr, dc):
        part = block
        if dr == -1:
            part = lax.slice_in_dim(part, rows - width, rows, axis=row_dim)
        elif dr == 1:
            part = lax.slice_in_dim(part, 0, width, axis=row_dim)
        if dc == -1:
            part = lax.slice_in_dim(part, cols - width, cols, axis=col_dim)
        elif dc == 1:
            part = lax.slice_in_dim(part, 0, width, axis=col_dim)
        if dr == 0:
            pairs = _grid_pairs(1, ncol, 0, dc, lambda r, c: c)
            return lax.ppermute(part, "col", pairs)
        if dc == 0:
            pairs = _grid_pairs(nrow, 1, dr, 0, lambda r, c: r)
            return lax.ppermute(part, "row", pairs)
        pairs = _grid_pairs(nrow, ncol, dr, dc, lambda r, c: r * ncol + c)
        return lax.ppermute(part, ("row", "col"), pairs)

    bands = []
    for dr in (-1, 0, 1):
        line = [block if (dr, dc) == (0, 0) else piece(dr, dc) for dc in (-1, 0, 1)]
        bands.append(jnp.concatenate(line, axis=col_dim))
    return jnp.concatenate(bands, axis=row_dim)


def lanczos_table():
    fraction = jnp.arange(NFRAC, dtype=jnp.float32) / NFRAC
    offset_grid = jnp.arange(-2, 4, dtype=jnp.float32)
    spread = offset_grid[None, :] - fraction[:, None]
    kernel = jnp.sinc(spread) * jnp.sinc(spread / 3.0)
    return kernel / jnp.sum(kernel, axis=1, keepdims=True)


def blur_table():
    offset_grid = jnp.arange(-PSF_RADIUS, PSF_RADIUS + 1, dtype=jnp.float32)
    widths = 0.7 + 0.2 * jnp.arange(NPSF, dtype=jnp.float32)
    kernel = jnp.exp(-0.5 * (offset_grid[None, :] / widths[:, None]) ** 2)
    return kernel / jnp.sum(kernel, axis=1, keepdims=True)


def lookup(indices, entries, kernel_table):
    chooser = (indices[:, None] == lax.broadcasted_iota(jnp.int32, (1, entries), 1)).astype(
        jnp.float32
    )
    return jnp.dot(chooser, kernel_table, precision=lax.Precision.HIGHEST)


def placed_taps(weights, shifts):
    reach = 2 * HALO + 1
    positions = lax.broadcasted_iota(jnp.int32, (1, 1, reach), 2)
    tap_slot = HALO + shifts[:, None, None] + lax.broadcasted_iota(jnp.int32, (1, 6, 1), 1) - 2
    spread = (tap_slot == positions).astype(jnp.float32)
    return jnp.sum(weights[:, :, None] * spread, axis=1)


def resample_axis(stack, coefficients, out_len, which_axis):
    out_shape = list(stack.shape)
    out_shape[which_axis] = out_len
    total = jnp.zeros(tuple(out_shape), jnp.float32)
    for position in range(2 * HALO + 1):
        window = lax.slice_in_dim(stack, position, position + out_len, 1, which_axis)
        total = total + coefficients[:, position, None, None] * window
    return total


def bisect_lower(valid_count, count_below):

    def one_pass(sweep_no, bounds):
        lower_edge, upper_edge = bounds
        middle = 0.5 * (lower_edge + upper_edge)
        enough = 2.0 * count_below(middle) >= valid_count
        return (jnp.where(enough, lower_edge, middle), jnp.where(enough, middle, upper_edge))

    initial = (
        jnp.full(valid_count.shape, -pivot_span, jnp.float32),
        jnp.full(valid_count.shape, pivot_span, jnp.float32),
    )
    return lax.fori_loop(0, PASSES, one_pass, initial)[0]


def stack_median(pixel_stack):
    valid_count = jnp.sum(pixel_stack < half_sentinel, axis=0, dtype=jnp.float32)

    def count_below(middle):
        return jnp.sum(pixel_stack <= middle[None], axis=0, dtype=jnp.float32)

    lower_edge = bisect_lower(valid_count, count_below)
    return jnp.min(jnp.where(pixel_stack > lower_edge[None], pixel_stack, sentinel), axis=0)


def body(exposures, bad_pixels, offsets, warp_index, blur_index):
    group_size, row_count, col_count = exposures.shape
    kernel_table = lanczos_table()
    coef_down = placed_taps(lookup(warp_index[:, 0], NFRAC, kernel_table), offsets[:, 0])
    coef_across = placed_taps(lookup(warp_index[:, 1], NFRAC, kernel_table), offsets[:, 1])
    padded = extended(exposures, 1, 2, HALO)
    across = resample_axis(padded, coef_down, row_count, 1)
    warped = resample_axis(across, coef_across, col_count, 2)
    flagged = jnp.where(bad_pixels == 1, sentinel, warped)
    band = stack_median(lax.all_to_all(flagged, "exp", split_axis=1, concat_axis=0, tiled=True))
    groups = lax.axis_size("exp")
    median_sky = lax.all_to_all(
        jnp.tile(band, (groups, 1)), "exp", split_axis=0, concat_axis=0, tiled=True
    )
    bordered = extended(median_sky, 0, 1, PSF_RADIUS)
    blur = blur_table()
    taps = 2 * PSF_RADIUS + 1
    blurred_rows = jnp.zeros((NPSF, row_count, col_count + 2 * PSF_RADIUS), jnp.float32)
    for tap_no in range(taps):
        blurred_rows = (
            blurred_rows
            + blur[:, tap_no, None, None] * bordered[None, tap_no : tap_no + row_count, :]
        )
    smoothed = jnp.zeros((NPSF, row_count, col_count), jnp.float32)
    for tap_no in range(taps):
        smoothed = (
            smoothed + blur[:, tap_no, None, None] * blurred_rows[:, :, tap_no : tap_no + col_count]
        )
    chooser = (blur_index[:, None] == lax.broadcasted_iota(jnp.int32, (1, NPSF), 1)).astype(
        jnp.float32
    )
    sky_model = jnp.zeros((group_size, row_count, col_count), jnp.float32)
    for kernel_no in range(NPSF):
        sky_model = sky_model + chooser[:, kernel_no, None, None] * smoothed[kernel_no][None]
    residual = jnp.where(bad_pixels == 1, 0.0, warped - sky_model)
    return (residual, median_sky)


def solution(mesh):
    return jax.shard_map(
        body,
        mesh=mesh,
        in_specs=(
            P("exp", "row", "col"),
            P("exp", "row", "col"),
            P("exp", None),
            P("exp", None),
            P("exp"),
        ),
        out_specs=(P("exp", "row", "col"), P("row", "col")),
        check_vma=False,
    )
```

profile of v0, /device:TPU:1, one launch (start us, length us, event | category | flops | bytes accessed | tf_op | source)
XLA Modules:
  0.0 119.1 jit_solution(8014442783377771152)
XLA Ops:
  0.6 1.8 %copy.37 = f32[16,32,512]{2,0,1:T(8,128)S(1)} copy(f32[16,32,512]{2,1,0:T(8,128)} %param.8) | data formatting | bytes 2097152 | tf_op args[0]
  2.6 5.6 %collective-permute-start = (f32[16,11,11]{2,0,1:T(8,128)S(1)}, f32[16,11,11]{2,0,1:T(8,128)S(1)}, u32[]{:S(2)}, u32[]{:S(2)}) collective-permute-start(f32[16,11,11]{2,0,1:T(8,128)S(1)} %get-tuple-element.118), channel_id=1, source_target_pairs={{0,3},{2,5},{4,7},{8,11},{10,13},{12,15},{16,19},{18,21},{20,23},{... | collective-permute-start | bytes 23240 | tf_op jit(solution)/shard_map/ppermute | solution.py:49
  8.2 1.3 %collective-permute-start.2 = (f32[16,11,11]{2,0,1:T(8,128)S(1)}, f32[16,11,11]{2,0,1:T(8,128)S(1)}, u32[]{:S(2)}, u32[]{:S(2)}) collective-permute-start(f32[16,11,11]{2,0,1:T(8,128)S(1)} %get-tuple-element.121), channel_id=1, source_target_pairs={{1,2},{3,4},{5,6},{9,10},{11,12},{13,14},{17,18},{19,20},{21,22},{... | collective-permute-start | bytes 23240 | tf_op jit(solution)/shard_map/ppermute | solution.py:49
  9.5 4.3 %collective-permute-start.5 = (f32[16,11,11]{2,0,1:T(8,128)S(1)}, f32[16,11,11]{2,0,1:T(8,128)S(1)}, u32[]{:S(2)}, u32[]{:S(2)}) collective-permute-start(f32[16,11,11]{2,0,1:T(8,128)S(1)} %get-tuple-element.120), channel_id=1, source_target_pairs={{2,1},{4,3},{6,5},{10,9},{12,11},{14,13},{18,17},{20,19},{22,21},{... | collective-permute-start | bytes 23240 | tf_op jit(solution)/shard_map/ppermute | solution.py:49
  13.8 2.8 %collective-permute-start.1 = (f32[16,11,512]{2,0,1:T(8,128)S(1)}, f32[16,11,512]{2,0,1:T(8,128)S(1)}, u32[]{:S(2)}, u32[]{:S(2)}) collective-permute-start(f32[16,11,512]{2,0,1:T(8,128)S(1)} %get-tuple-element.122), channel_id=1, source_target_pairs={{0,2},{2,4},{4,6},{1,3},{3,5},{5,7},{8,10},{10,12},{12,14},{9,11},... | collective-permute-start | bytes 1081352 | tf_op jit(solution)/shard_map/ppermute | solution.py:47
  16.7 1.9 %collective-permute-start.6 = (f32[16,11,512]{2,0,1:T(8,128)S(1)}, f32[16,11,512]{2,0,1:T(8,128)S(1)}, u32[]{:S(2)}, u32[]{:S(2)}) collective-permute-start(f32[16,11,512]{2,0,1:T(8,128)S(1)} %get-tuple-element.123), channel_id=1, source_target_pairs={{2,0},{4,2},{6,4},{3,1},{5,3},{7,5},{10,8},{12,10},{14,12},{11,9},... | collective-permute-start | bytes 1081352 | tf_op jit(solution)/shard_map/ppermute | solution.py:47
  18.9 0.2 fusion.64
  19.1 0.2 fusion.63
  19.5 0.5 slice_reduce_fusion.44
  20.0 0.5 slice_reduce_fusion.45
  20.5 0.2 slice_reduce_fusion.43
  20.8 1.3 %collective-permute-start.7 = (f32[16,11,11]{2,0,1:T(8,128)S(1)}, f32[16,11,11]{2,0,1:T(8,128)S(1)}, u32[]{:S(2)}, u32[]{:S(2)}) collective-permute-start(f32[16,11,11]{2,0,1:T(8,128)S(1)} %get-tuple-element.119), channel_id=1, source_target_pairs={{3,0},{5,2},{7,4},{11,8},{13,10},{15,12},{19,16},{21,18},{23,20},{... | collective-permute-start | bytes 23240 | tf_op jit(solution)/shard_map/ppermute | solution.py:49
  22.1 2.9 %collective-permute-start.3 = (f32[16,32,11]{2,0,1:T(8,128)S(1)}, f32[16,32,11]{2,0,1:T(8,128)S(1)}, u32[]{:S(2)}, u32[]{:S(2)}) collective-permute-start(f32[16,32,11]{2,0,1:T(8,128)S(1)} %get-tuple-element.124), channel_id=1, source_target_pairs={{0,1},{2,3},{4,5},{6,7},{8,9},{10,11},{12,13},{14,15},{16,17},{18,... | collective-permute-start | bytes 67592 | tf_op jit(solution)/shard_map/ppermute | solution.py:44
  25.0 1.3 %collective-permute-start.4 = (f32[16,32,11]{2,0,1:T(8,128)S(1)}, f32[16,32,11]{2,0,1:T(8,128)S(1)}, u32[]{:S(2)}, u32[]{:S(2)}) collective-permute-start(f32[16,32,11]{2,0,1:T(8,128)S(1)} %get-tuple-element.125), channel_id=1, source_target_pairs={{1,0},{3,2},{5,4},{7,6},{9,8},{11,10},{13,12},{15,14},{17,16},{19,... | collective-permute-start | bytes 67592 | tf_op jit(solution)/shard_map/ppermute | solution.py:44
  26.3 0.2 slice_reduce_fusion.21
  26.5 2.0 %collective-permute-done.7 = f32[16,11,11]{2,0,1:T(8,128)S(1)} collective-permute-done((f32[16,11,11]{2,0,1:T(8,128)S(1)}, f32[16,11,11]{2,0,1:T(8,128)S(1)}, u32[]{:S(2)}, u32[]{:S(2)}) %collective-permute-start.7) | collective-permute-done | bytes 7776 | tf_op jit(solution)/shard_map/ppermute | solution.py:49
  28.5 0.2 collective-permute-done.3
  28.7 4.1 %collective-permute-done.4 = f32[16,32,11]{2,0,1:T(8,128)S(1)} collective-permute-done((f32[16,32,11]{2,0,1:T(8,128)S(1)}, f32[16,32,11]{2,0,1:T(8,128)S(1)}, u32[]{:S(2)}, u32[]{:S(2)}) %collective-permute-start.4) | collective-permute-done | bytes 22560 | tf_op jit(solution)/shard_map/ppermute | solution.py:44
  32.8 1.2 maximum_maximum_fusion
  34.0 3.3 %fusion = f32[16,32,534]{2,0,1:T(8,128)S(1)} fusion(f32[16,43,534]{2,0,1:T(8,128)S(1)} %get-tuple-element.117, f32[16,43,534]{2,0,1:T(8,128)S(1)} %get-tuple-element.116, f32[16,32,11]{2,0,1:T(8,128)S(1)} %collective-permute-done.4, f32[16,32,512]{2,0,1:T(8,128)S(1)} %copy.37, f32[16,32,11]{2,0,1:T(8,128)S(1)} %collective-permute-done.3, ...), kind=kLoop, calls=%fused_computation.9 | loop fusion | flops 12850176 | bytes 26248640 | tf_op jit(solution)/shard_map/add | solution.py:94
  37.3 7.0 %broadcast_select_fusion = (f32[16,32,512]{2,0,1:T(8,128)}, f32[16,32,512]{2,0,1:T(8,128)S(1)}, pred[16,32,512]{2,0,1:T(8,128)(4,1)S(1)}) fusion(f32[16,32,534]{2,0,1:T(8,128)S(1)} %fusion, f32[16]{0:T(128)S(1)} %get-tuple-element.56, f32[16]{0:T(128)S(1)} %get-tuple-element.57, f32[16]{0:T(128)S(1)} %get-tuple-element.58, f32[16]{0:T(128)S(1)} %get-tuple-element.59, ...), kind=kLoop, calls=%fused_computation.120 | loop fusion | flops 12320768 | bytes 27526592 | tf_op jit(solution)/shard_map/jit(_where)/select_n | solution.py:131
  44.3 4.7 %all-to-all-start = ((f32[16,32,512]{2,0,1:T(8,128)}), f32[16,32,512]{2,0,1:T(8,128)S(1)}, u32[]{:S(2)}, u32[]{:S(2)}) async-start(f32[16,32,512]{2,0,1:T(8,128)} %get-tuple-element.113), calls=%async_computation | async-start | bytes 2097152 | tf_op jit(solution)/shard_map/all_to_all | solution.py:132
  49.2 25.1 %all-to-all-done = f32[16,32,512]{2,0,1:T(8,128)S(1)} async-done(((f32[16,32,512]{2,0,1:T(8,128)}), f32[16,32,512]{2,0,1:T(8,128)S(1)}, u32[]{:S(2)}, u32[]{:S(2)}) %all-to-all-start) | async-done | bytes 1048608 | tf_op jit(solution)/shard_map/all_to_all | solution.py:132
  74.3 0.6 copy.46
  74.9 0.1 convert_reduce_fusion.1
  75.1 3.6 %while.13 = (s32[]{:T(128)}, f32[8,512]{1,0:T(8,128)S(1)}, f32[8,512]{1,0:T(8,128)S(1)}, f32[64,8,512]{2,1,0:T(8,128)S(1)}, f32[8,512]{1,0:T(8,128)S(1)}, /*index=5*/s32[]{:T(128)}, s32[]{:T(128)}) while((s32[]{:T(128)}, f32[8,512]{1,0:T(8,128)S(1)}, f32[8,512]{1,0:T(8,128)S(1)}, f32[64,8,512]{2,1,0:T(8,128)S(1)}, ...), condition=%wide.region_7.9_spmd.clone, body=%wide.region_5.8_spmd.clone.sunk | while | flops 1110019 | bytes 1302617 | solution.py:110
  75.1 0.1 convert_reduce_fusion.3
  75.3 0.1 convert_reduce_fusion.3
  76.0 0.1 convert_reduce_fusion.3
  76.3 0.1 convert_reduce_fusion.3
  78.7 0.2 fusion.22
  78.9 0.6 tile.2
  79.5 3.3 %all-to-all-start.1 = ((f32[4,8,512]{2,1,0:T(8,128)}), f32[4,8,512]{2,1,0:T(8,128)S(1)}, u32[]{:S(2)}, u32[]{:S(2)}) async-start(f32[4,8,512]{2,1,0:T(8,128)} %tile.2), calls=%async_computation.1 | async-start | bytes 131072 | tf_op jit(solution)/shard_map/all_to_all | solution.py:134
  82.8 4.5 %all-to-all-done.1 = f32[4,8,512]{2,1,0:T(8,128)S(1)} async-done(((f32[4,8,512]{2,1,0:T(8,128)}), f32[4,8,512]{2,1,0:T(8,128)S(1)}, u32[]{:S(2)}, u32[]{:S(2)}) %all-to-all-start.1) | async-done | bytes 65568 | tf_op jit(solution)/shard_map/all_to_all | solution.py:134
  87.4 1.5 %collective-permute-start.11 = (f32[32,4]{1,0:T(8,128)S(1)}, f32[32,4]{1,0:T(8,128)S(1)}, u32[]{:S(2)}, u32[]{:S(2)}) collective-permute-start(f32[32,4]{1,0:T(8,128)S(1)} %get-tuple-element.150), channel_id=1, source_target_pairs={{0,1},{2,3},{4,5},{6,7},{8,9},{10,11},{12,13},{14,15},{16,17},{18,... | collective-permute-start | bytes 1544 | tf_op jit(solution)/shard_map/ppermute | solution.py:44
  89.0 1.3 %collective-permute-start.12 = (f32[32,4]{1,0:T(8,128)S(1)}, f32[32,4]{1,0:T(8,128)S(1)}, u32[]{:S(2)}, u32[]{:S(2)}) collective-permute-start(f32[32,4]{1,0:T(8,128)S(1)} %get-tuple-element.151), channel_id=1, source_target_pairs={{1,0},{3,2},{5,4},{7,6},{9,8},{11,10},{13,12},{15,14},{17,16},{19,... | collective-permute-start | bytes 1544 | tf_op jit(solution)/shard_map/ppermute | solution.py:44
  90.3 2.9 %collective-permute-start.14 = (f32[4,512]{1,0:T(4,128)S(1)}, f32[4,512]{1,0:T(4,128)S(1)}, u32[]{:S(2)}, u32[]{:S(2)}) collective-permute-start(f32[4,512]{1,0:T(4,128)S(1)} %get-tuple-element.149), channel_id=1, source_target_pairs={{2,0},{4,2},{6,4},{3,1},{5,3},{7,5},{10,8},{12,10},{14,12},{11,9},... | collective-permute-start | bytes 24584 | tf_op jit(solution)/shard_map/ppermute | solution.py:47
  93.2 8.0 %collective-permute-start.9 = (f32[4,512]{1,0:T(4,128)S(1)}, f32[4,512]{1,0:T(4,128)S(1)}, u32[]{:S(2)}, u32[]{:S(2)}) collective-permute-start(f32[4,512]{1,0:T(4,128)S(1)} %get-tuple-element.148), channel_id=1, source_target_pairs={{0,2},{2,4},{4,6},{1,3},{3,5},{5,7},{8,10},{10,12},{12,14},{9,11},... | collective-permute-start | bytes 24584 | tf_op jit(solution)/shard_map/ppermute | solution.py:47
  101.2 1.3 %collective-permute-start.10 = (f32[4,4]{1,0:T(4,128)S(1)}, f32[4,4]{1,0:T(4,128)S(1)}, u32[]{:S(2)}, u32[]{:S(2)}) collective-permute-start(f32[4,4]{1,0:T(4,128)S(1)} %get-tuple-element.147), channel_id=1, source_target_pairs={{1,2},{3,4},{5,6},{9,10},{11,12},{13,14},{17,18},{19,20},{21,22},{... | collective-permute-start | bytes 200 | tf_op jit(solution)/shard_map/ppermute | solution.py:49
  102.5 4.3 %collective-permute-start.13 = (f32[4,4]{1,0:T(4,128)S(1)}, f32[4,4]{1,0:T(4,128)S(1)}, u32[]{:S(2)}, u32[]{:S(2)}) collective-permute-start(f32[4,4]{1,0:T(4,128)S(1)} %get-tuple-element.146), channel_id=1, source_target_pairs={{2,1},{4,3},{6,5},{10,9},{12,11},{14,13},{18,17},{20,19},{22,21},{... | collective-permute-start | bytes 200 | tf_op jit(solution)/shard_map/ppermute | solution.py:49
  106.8 1.3 %collective-permute-start.15 = (f32[4,4]{1,0:T(4,128)S(1)}, f32[4,4]{1,0:T(4,128)S(1)}, u32[]{:S(2)}, u32[]{:S(2)}) collective-permute-start(f32[4,4]{1,0:T(4,128)S(1)} %get-tuple-element.145), channel_id=1, source_target_pairs={{3,0},{5,2},{7,4},{11,8},{13,10},{15,12},{19,16},{21,18},{23,20},{... | collective-permute-start | bytes 200 | tf_op jit(solution)/shard_map/ppermute | solution.py:49
  108.2 5.3 %collective-permute-start.8 = (f32[4,4]{1,0:T(4,128)S(1)}, f32[4,4]{1,0:T(4,128)S(1)}, u32[]{:S(2)}, u32[]{:S(2)}) collective-permute-start(f32[4,4]{1,0:T(4,128)S(1)} %get-tuple-element.144), channel_id=1, source_target_pairs={{0,3},{2,5},{4,7},{8,11},{10,13},{12,15},{16,19},{18,21},{20,23},{... | collective-permute-start | bytes 200 | tf_op jit(solution)/shard_map/ppermute | solution.py:49
  113.6 0.5 collective-permute-done.8
  114.3 0.6 multiply_add_fusion
  114.9 1.3 %fusion.45 = f32[8,32,512]{2,1,0:T(8,128)S(1)} fusion(f32[8,32,520]{2,1,0:T(8,128)S(1)} %multiply_add_fusion, f32[8]{0:T(128)S(1)} %get-tuple-element.153, f32[8]{0:T(128)S(1)} %get-tuple-element.154, f32[8]{0:T(128)S(1)} %get-tuple-element.155, f32[8]{0:T(128)S(1)} %get-tuple-element.156, f32[8]{0:T(128)S(1)} %get-tuple-element.157, ...), kind=kLoop, calls=%fused_computation.104 | loop fusion | flops 2228224 | bytes 5243168 | tf_op jit(solution)/shard_map/add | solution.py:149
  116.2 0.7 subtract_select_fusion
  116.9 1.6 %copy.47 = f32[16,32,512]{2,1,0:T(8,128)} copy(f32[16,32,512]{2,0,1:T(8,128)S(1)} %subtract_select_fusion) | data formatting | bytes 2097152
  118.5 0.6 copy.60
  (124 shorter events, 3.7 us)
Async XLA Ops:
  2.6 16.2 %copy-start.1 = (s32[16,2]{0,1:T(2,128)S(1)}, s32[16,2]{0,1:T(2,128)}, u32[]{:S(2)}) copy-start(s32[16,2]{0,1:T(2,128)} %param.11) | copy-start | bytes 388
  2.6 16.2 %copy-start.2 = (s32[16,2]{0,1:T(2,128)S(1)}, s32[16,2]{0,1:T(2,128)}, u32[]{:S(2)}) copy-start(s32[16,2]{0,1:T(2,128)} %param.10) | copy-start | bytes 388
  2.6 18.2 %collective-permute-start = (f32[16,11,11]{2,0,1:T(8,128)S(1)}, f32[16,11,11]{2,0,1:T(8,128)S(1)}, u32[]{:S(2)}, u32[]{:S(2)}) collective-permute-start(f32[16,11,11]{2,0,1:T(8,128)S(1)} %get-tuple-element.118), channel_id=1, source_target_pairs={{0,3},{2,5},{4,7},{8,11},{10,13},{12,15},{16,19},{18,21},{20,23},{... | collective-permute-start | bytes 23240 | tf_op jit(solution)/shard_map/ppermute | solution.py:49
  8.2 13.9 %collective-permute-start.2 = (f32[16,11,11]{2,0,1:T(8,128)S(1)}, f32[16,11,11]{2,0,1:T(8,128)S(1)}, u32[]{:S(2)}, u32[]{:S(2)}) collective-permute-start(f32[16,11,11]{2,0,1:T(8,128)S(1)} %get-tuple-element.121), channel_id=1, source_target_pairs={{1,2},{3,4},{5,6},{9,10},{11,12},{13,14},{17,18},{19,20},{21,22},{... | collective-permute-start | bytes 23240 | tf_op jit(solution)/shard_map/ppermute | solution.py:49
  9.5 15.5 %collective-permute-start.5 = (f32[16,11,11]{2,0,1:T(8,128)S(1)}, f32[16,11,11]{2,0,1:T(8,128)S(1)}, u32[]{:S(2)}, u32[]{:S(2)}) collective-permute-start(f32[16,11,11]{2,0,1:T(8,128)S(1)} %get-tuple-element.120), channel_id=1, source_target_pairs={{2,1},{4,3},{6,5},{10,9},{12,11},{14,13},{18,17},{20,19},{22,21},{... | collective-permute-start | bytes 23240 | tf_op jit(solution)/shard_map/ppermute | solution.py:49
  13.8 18.9 %collective-permute-start.1 = (f32[16,11,512]{2,0,1:T(8,128)S(1)}, f32[16,11,512]{2,0,1:T(8,128)S(1)}, u32[]{:S(2)}, u32[]{:S(2)}) collective-permute-start(f32[16,11,512]{2,0,1:T(8,128)S(1)} %get-tuple-element.122), channel_id=1, source_target_pairs={{0,2},{2,4},{4,6},{1,3},{3,5},{5,7},{8,10},{10,12},{12,14},{9,11},... | collective-permute-start | bytes 1081352 | tf_op jit(solution)/shard_map/ppermute | solution.py:47
  16.7 16.1 %collective-permute-start.6 = (f32[16,11,512]{2,0,1:T(8,128)S(1)}, f32[16,11,512]{2,0,1:T(8,128)S(1)}, u32[]{:S(2)}, u32[]{:S(2)}) collective-permute-start(f32[16,11,512]{2,0,1:T(8,128)S(1)} %get-tuple-element.123), channel_id=1, source_target_pairs={{2,0},{4,2},{6,4},{3,1},{5,3},{7,5},{10,8},{12,10},{14,12},{11,9},... | collective-permute-start | bytes 1081352 | tf_op jit(solution)/shard_map/ppermute | solution.py:47
  20.8 7.7 %collective-permute-start.7 = (f32[16,11,11]{2,0,1:T(8,128)S(1)}, f32[16,11,11]{2,0,1:T(8,128)S(1)}, u32[]{:S(2)}, u32[]{:S(2)}) collective-permute-start(f32[16,11,11]{2,0,1:T(8,128)S(1)} %get-tuple-element.119), channel_id=1, source_target_pairs={{3,0},{5,2},{7,4},{11,8},{13,10},{15,12},{19,16},{21,18},{23,20},{... | collective-permute-start | bytes 23240 | tf_op jit(solution)/shard_map/ppermute | solution.py:49
  22.1 6.6 %collective-permute-start.3 = (f32[16,32,11]{2,0,1:T(8,128)S(1)}, f32[16,32,11]{2,0,1:T(8,128)S(1)}, u32[]{:S(2)}, u32[]{:S(2)}) collective-permute-start(f32[16,32,11]{2,0,1:T(8,128)S(1)} %get-tuple-element.124), channel_id=1, source_target_pairs={{0,1},{2,3},{4,5},{6,7},{8,9},{10,11},{12,13},{14,15},{16,17},{18,... | collective-permute-start | bytes 67592 | tf_op jit(solution)/shard_map/ppermute | solution.py:44
  25.0 7.8 %collective-permute-start.4 = (f32[16,32,11]{2,0,1:T(8,128)S(1)}, f32[16,32,11]{2,0,1:T(8,128)S(1)}, u32[]{:S(2)}, u32[]{:S(2)}) collective-permute-start(f32[16,32,11]{2,0,1:T(8,128)S(1)} %get-tuple-element.125), channel_id=1, source_target_pairs={{1,0},{3,2},{5,4},{7,6},{9,8},{11,10},{13,12},{15,14},{17,16},{19,... | collective-permute-start | bytes 67592 | tf_op jit(solution)/shard_map/ppermute | solution.py:44
  33.9 3.3 %copy-start = (s32[16,32,512]{2,1,0:T(8,128)S(1)}, s32[16,32,512]{2,1,0:T(8,128)}, u32[]{:S(2)}) copy-start(s32[16,32,512]{2,1,0:T(8,128)} %param.9) | copy-start | bytes 3145732
  44.3 4.8 %copy-start.3 = (s32[16]{0:T(128)S(1)}, s32[16]{0:T(128)}, u32[]{:S(2)}) copy-start(s32[16]{0:T(128)} %param.12) | copy-start | bytes 196
  44.3 30.0 %all-to-all-start = ((f32[16,32,512]{2,0,1:T(8,128)}), f32[16,32,512]{2,0,1:T(8,128)S(1)}, u32[]{:S(2)}, u32[]{:S(2)}) async-start(f32[16,32,512]{2,0,1:T(8,128)} %get-tuple-element.113), calls=%async_computation | async-start | bytes 2097152 | tf_op jit(solution)/shard_map/all_to_all | solution.py:132
  79.5 7.9 %all-to-all-start.1 = ((f32[4,8,512]{2,1,0:T(8,128)}), f32[4,8,512]{2,1,0:T(8,128)S(1)}, u32[]{:S(2)}, u32[]{:S(2)}) async-start(f32[4,8,512]{2,1,0:T(8,128)} %tile.2), calls=%async_computation.1 | async-start | bytes 131072 | tf_op jit(solution)/shard_map/all_to_all | solution.py:134
  87.4 15.1 %collective-permute-start.11 = (f32[32,4]{1,0:T(8,128)S(1)}, f32[32,4]{1,0:T(8,128)S(1)}, u32[]{:S(2)}, u32[]{:S(2)}) collective-permute-start(f32[32,4]{1,0:T(8,128)S(1)} %get-tuple-element.150), channel_id=1, source_target_pairs={{0,1},{2,3},{4,5},{6,7},{8,9},{10,11},{12,13},{14,15},{16,17},{18,... | collective-permute-start | bytes 1544 | tf_op jit(solution)/shard_map/ppermute | solution.py:44
  89.0 17.8 %collective-permute-start.12 = (f32[32,4]{1,0:T(8,128)S(1)}, f32[32,4]{1,0:T(8,128)S(1)}, u32[]{:S(2)}, u32[]{:S(2)}) collective-permute-start(f32[32,4]{1,0:T(8,128)S(1)} %get-tuple-element.151), channel_id=1, source_target_pairs={{1,0},{3,2},{5,4},{7,6},{9,8},{11,10},{13,12},{15,14},{17,16},{19,... | collective-permute-start | bytes 1544 | tf_op jit(solution)/shard_map/ppermute | solution.py:44
  90.3 23.8 %collective-permute-start.14 = (f32[4,512]{1,0:T(4,128)S(1)}, f32[4,512]{1,0:T(4,128)S(1)}, u32[]{:S(2)}, u32[]{:S(2)}) collective-permute-start(f32[4,512]{1,0:T(4,128)S(1)} %get-tuple-element.149), channel_id=1, source_target_pairs={{2,0},{4,2},{6,4},{3,1},{5,3},{7,5},{10,8},{12,10},{14,12},{11,9},... | collective-permute-start | bytes 24584 | tf_op jit(solution)/shard_map/ppermute | solution.py:47
  93.2 20.9 %collective-permute-start.9 = (f32[4,512]{1,0:T(4,128)S(1)}, f32[4,512]{1,0:T(4,128)S(1)}, u32[]{:S(2)}, u32[]{:S(2)}) collective-permute-start(f32[4,512]{1,0:T(4,128)S(1)} %get-tuple-element.148), channel_id=1, source_target_pairs={{0,2},{2,4},{4,6},{1,3},{3,5},{5,7},{8,10},{10,12},{12,14},{9,11},... | collective-permute-start | bytes 24584 | tf_op jit(solution)/shard_map/ppermute | solution.py:47
  101.2 7.0 %collective-permute-start.10 = (f32[4,4]{1,0:T(4,128)S(1)}, f32[4,4]{1,0:T(4,128)S(1)}, u32[]{:S(2)}, u32[]{:S(2)}) collective-permute-start(f32[4,4]{1,0:T(4,128)S(1)} %get-tuple-element.147), channel_id=1, source_target_pairs={{1,2},{3,4},{5,6},{9,10},{11,12},{13,14},{17,18},{19,20},{21,22},{... | collective-permute-start | bytes 200 | tf_op jit(solution)/shard_map/ppermute | solution.py:49
  102.5 11.0 %collective-permute-start.13 = (f32[4,4]{1,0:T(4,128)S(1)}, f32[4,4]{1,0:T(4,128)S(1)}, u32[]{:S(2)}, u32[]{:S(2)}) collective-permute-start(f32[4,4]{1,0:T(4,128)S(1)} %get-tuple-element.146), channel_id=1, source_target_pairs={{2,1},{4,3},{6,5},{10,9},{12,11},{14,13},{18,17},{20,19},{22,21},{... | collective-permute-start | bytes 200 | tf_op jit(solution)/shard_map/ppermute | solution.py:49
  106.8 6.8 %collective-permute-start.15 = (f32[4,4]{1,0:T(4,128)S(1)}, f32[4,4]{1,0:T(4,128)S(1)}, u32[]{:S(2)}, u32[]{:S(2)}) collective-permute-start(f32[4,4]{1,0:T(4,128)S(1)} %get-tuple-element.145), channel_id=1, source_target_pairs={{3,0},{5,2},{7,4},{11,8},{13,10},{15,12},{19,16},{21,18},{23,20},{... | collective-permute-start | bytes 200 | tf_op jit(solution)/shard_map/ppermute | solution.py:49
  108.2 5.9 %collective-permute-start.8 = (f32[4,4]{1,0:T(4,128)S(1)}, f32[4,4]{1,0:T(4,128)S(1)}, u32[]{:S(2)}, u32[]{:S(2)}) collective-permute-start(f32[4,4]{1,0:T(4,128)S(1)} %get-tuple-element.144), channel_id=1, source_target_pairs={{0,3},{2,5},{4,7},{8,11},{10,13},{12,15},{16,19},{18,21},{20,23},{... | collective-permute-start | bytes 200 | tf_op jit(solution)/shard_map/ppermute | solution.py:49
where the time goes:
time: 120 us; the launch traced here: 119 us
  starting transfers between devices  55.2 us (46%)
  waiting for transfers between devices  36.5 us (30%)
  other arithmetic  17.9 us (15%)
  local copies, waits for them, and re-layouts  7.33 us (6%)
    all_to_all x1, waiting for transfers between devices, body(): lax.all_to_all(flagged, 'exp', split_axis=1, concat_axis=0, tiled=True)  25.1 us
    ppermute x8, starting transfers between devices, piece(): return lax.ppermute(part, ('row', 'col'), pairs)  24.6 us
    ppermute x4, starting transfers between devices, piece(): return lax.ppermute(part, 'row', pairs)  15.6 us
    select_n x1, other arithmetic, body(): flagged = jnp.where(bad_pixels == 1, sentinel, warped)  6.99 us
    ppermute x4, starting transfers between devices, piece(): return lax.ppermute(part, 'col', pairs)  6.92 us
    all_to_all x1, starting transfers between devices, body(): lax.all_to_all(flagged, 'exp', split_axis=1, concat_axis=0, tiled=True)  4.72 us
    all_to_all x1, waiting for transfers between devices, body(): lax.all_to_all(jnp.tile(band, (groups, 1)), 'exp', split_axis=0, concat_a...  4.55 us
    ppermute x4, waiting for transfers between devices, piece(): return lax.ppermute(part, 'col', pairs)  4.33 us
  transfers between devices with their start and end apart: 18, of which 6 were waited for; matrix products, arithmetic and copies ran while one was open for 2% of the time, Pallas kernels for 0%

commit v1 on v0

--- a/solution.py
+++ b/solution.py
@@ -1,3 +1,4 @@
+import functools
 import jax
 import jax.numpy as jnp
 from jax import lax
@@ -11,6 +12,36 @@
 sentinel = 1000000.0
 half_sentinel = 500000.0
 pivot_span = 16.0
+
+
+def treat_scales_for(z, which_dim, piece_in):
+    all_rows, x_now = (z.shape[:which_dim], z.shape[which_dim + 1 :])
+    finding = z.reshape(*all_rows, piece_in, -1, *x_now)
+    return jnp.moveaxis(finding, which_dim, 0)
+
+
+def _supply_loads(page, dimension_no):
+    main = list(page.shape[1:])
+    main[dimension_no] *= page.shape[0]
+    return jnp.moveaxis(page, 0, dimension_no).reshape(main)
+
+
+def scan_series_all(own_rows, dev_axis, local_block, array_in):
+    low = lax.psum(1, dev_axis)
+    front = lax.axis_index(dev_axis)
+    a_next, block_next = (low, front)
+    row_out = treat_scales_for(own_rows, local_block, a_next)
+    buffers = [row_out[block_next]]
+    for s in range(1, a_next):
+        spare = row_out[block_next ^ s]
+        res = lax.ppermute(spare, dev_axis, [(t, t ^ s) for t in range(a_next)])
+        buffers.append(res)
+    ready = jnp.stack(buffers, axis=0)
+    row_out = ready[block_next ^ jnp.arange(a_next)]
+    return _supply_loads(row_out, array_in)
+
+
+post_scales_for = functools.partial(scan_series_all, dev_axis="exp", local_block=1, array_in=0)
 
 
 def _grid_pairs(nrow, ncol, dr, dc, flat):
@@ -129,7 +160,7 @@
     across = resample_axis(padded, coef_down, row_count, 1)
     warped = resample_axis(across, coef_across, col_count, 2)
     flagged = jnp.where(bad_pixels == 1, sentinel, warped)
-    band = stack_median(lax.all_to_all(flagged, "exp", split_axis=1, concat_axis=0, tiled=True))
+    band = stack_median(post_scales_for(flagged))
     groups = lax.axis_size("exp")
     median_sky = lax.all_to_all(
         jnp.tile(band, (groups, 1)), "exp", split_axis=0, concat_axis=0, tiled=True

time: 120 us -> 126 us (1.050)
  the two profiles are of different devices: /device:TPU:1 before, /device:TPU:3 now
where the time goes in v1:
time: 126 us; the launch traced here: 125 us
  starting transfers between devices  44.9 us (36%)
  waiting for transfers between devices  40.3 us (32%)
  other arithmetic  26 us (21%)
  local copies, waits for them, and re-layouts  11.3 us (9%)
  between operations  1.68 us (1%)
    ppermute x8, starting transfers between devices, piece(): return lax.ppermute(part, ('row', 'col'), pairs)  24.8 us
    ppermute x3, waiting for transfers between devices, scan_series_all(): res = lax.ppermute(spare, dev_axis, [(t, t ^ s) for t in range(a_next)])  20.7 us
    ppermute x8, waiting for transfers between devices, piece(): return lax.ppermute(part, ('row', 'col'), pairs)  14.6 us
    ppermute x4, starting transfers between devices, piece(): return lax.ppermute(part, 'row', pairs)  7.79 us
    reshape x1, other arithmetic, treat_scales_for(): finding = z.reshape(*all_rows, piece_in, -1, *x_now)  7.55 us
    add x1, other arithmetic, resample_axis(): total = total + coefficients[:, position, None, None] * window  5.85 us
    ppermute x4, starting transfers between devices, piece(): return lax.ppermute(part, 'col', pairs)  5.14 us
    all_to_all x1, waiting for transfers between devices, body(): lax.all_to_all(jnp.tile(band, (groups, 1)), 'exp', split_axis=0, concat_a...  5 us
  transfers between devices with their start and end apart: 20, of which 5 were waited for; matrix products, arithmetic and copies ran while one was open for 6% of the time, Pallas kernels for 0%

profile of v1, /device:TPU:3, one launch (start us, length us, event | category | flops | bytes accessed | tf_op | source)
XLA Modules:
  0.0 125.3 jit_solution(16536986357728254833)
XLA Ops:
  0.6 2.0 %fusion.132 = (f32[16,11,11]{2,1,0:T(8,128)S(1)}, f32[16,11,11]{2,1,0:T(8,128)}, f32[16,11,11]{2,1,0:T(8,128)S(1)}, f32[16,11,11]{2,1,0:T(8,128)}) fusion(f32[16,32,512]{2,1,0:T(8,128)} %param.8), kind=kLoop, calls=%fused_computation.314 | loop fusion | bytes 61952 | tf_op jit(solution)/shard_map/slice | solution.py:70
  2.6 3.8 %collective-permute-start.2 = (f32[16,11,11]{2,1,0:T(8,128)S(1)}, f32[16,11,11]{2,1,0:T(8,128)S(1)}, u32[]{:S(2)}, u32[]{:S(2)}) collective-permute-start(f32[16,11,11]{2,1,0:T(8,128)S(1)} %get-tuple-element.118), channel_id=1, source_target_pairs={{1,2},{3,4},{5,6},{9,10},{11,12},{13,14},{17,18},{19,20},{21,22},{... | collective-permute-start | bytes 23240 | tf_op jit(solution)/shard_map/ppermute | solution.py:80
  6.4 0.9 fusion.133
  7.4 2.0 %collective-permute-start.1 = (f32[16,11,512]{2,1,0:T(8,128)}, f32[16,11,512]{2,1,0:T(8,128)S(1)}, u32[]{:S(2)}, u32[]{:S(2)}) collective-permute-start(f32[16,11,512]{2,1,0:T(8,128)} %get-tuple-element.120), channel_id=1, source_target_pairs={{0,2},{2,4},{4,6},{1,3},{3,5},{5,7},{8,10},{10,12},{12,14},{9,11},... | collective-permute-start | bytes 1081352 | tf_op jit(solution)/shard_map/ppermute | solution.py:78
  9.4 1.3 %collective-permute-start = (f32[16,11,11]{2,1,0:T(8,128)S(1)}, f32[16,11,11]{2,1,0:T(8,128)S(1)}, u32[]{:S(2)}, u32[]{:S(2)}) collective-permute-start(f32[16,11,11]{2,1,0:T(8,128)S(1)} %get-tuple-element.116), channel_id=1, source_target_pairs={{0,3},{2,5},{4,7},{8,11},{10,13},{12,15},{16,19},{18,21},{20,23},{... | collective-permute-start | bytes 23240 | tf_op jit(solution)/shard_map/ppermute | solution.py:80
  10.7 4.9 %collective-permute-start.7 = (f32[16,11,11]{2,1,0:T(8,128)}, f32[16,11,11]{2,1,0:T(8,128)}, u32[]{:S(2)}, u32[]{:S(2)}) collective-permute-start(f32[16,11,11]{2,1,0:T(8,128)} %get-tuple-element.119), channel_id=1, source_target_pairs={{3,0},{5,2},{7,4},{11,8},{13,10},{15,12},{19,16},{21,18},{23,20},{... | collective-permute-start | bytes 23240 | tf_op jit(solution)/shard_map/ppermute | solution.py:80
  15.6 1.9 %collective-permute-start.6 = (f32[16,11,512]{2,1,0:T(8,128)S(1)}, f32[16,11,512]{2,1,0:T(8,128)S(1)}, u32[]{:S(2)}, u32[]{:S(2)}) collective-permute-start(f32[16,11,512]{2,1,0:T(8,128)S(1)} %get-tuple-element.121), channel_id=1, source_target_pairs={{2,0},{4,2},{6,4},{3,1},{5,3},{7,5},{10,8},{12,10},{14,12},{11,9},... | collective-permute-start | bytes 1081352 | tf_op jit(solution)/shard_map/ppermute | solution.py:78
  17.6 0.8 fusion.134
  18.5 0.2 fusion.64
  18.8 1.1 slice_reduce_fusion.44
  19.9 0.2 fusion.63
  20.4 0.8 slice_reduce_fusion.43
  21.2 1.1 slice_reduce_fusion.45
  22.3 0.8 slice_reduce_fusion.21
  23.1 1.3 %collective-permute-start.4 = (f32[16,32,11]{2,1,0:T(8,128)}, f32[16,32,11]{2,1,0:T(8,128)S(1)}, u32[]{:S(2)}, u32[]{:S(2)}) collective-permute-start(f32[16,32,11]{2,1,0:T(8,128)} %get-tuple-element.123), channel_id=1, source_target_pairs={{1,0},{3,2},{5,4},{7,6},{9,8},{11,10},{13,12},{15,14},{17,16},{19,... | collective-permute-start | bytes 67592 | tf_op jit(solution)/shard_map/ppermute | solution.py:75
  24.4 0.6 copy-done.5
  25.0 1.3 %collective-permute-start.3 = (f32[16,32,11]{2,1,0:T(8,128)S(1)}, f32[16,32,11]{2,1,0:T(8,128)S(1)}, u32[]{:S(2)}, u32[]{:S(2)}) collective-permute-start(f32[16,32,11]{2,1,0:T(8,128)S(1)} %get-tuple-element.122), channel_id=1, source_target_pairs={{0,1},{2,3},{4,5},{6,7},{8,9},{10,11},{12,13},{14,15},{16,17},{18,... | collective-permute-start | bytes 67592 | tf_op jit(solution)/shard_map/ppermute | solution.py:75
  26.3 1.3 %collective-permute-start.5 = (f32[16,11,11]{2,1,0:T(8,128)}, f32[16,11,11]{2,1,0:T(8,128)}, u32[]{:S(2)}, u32[]{:S(2)}) collective-permute-start(f32[16,11,11]{2,1,0:T(8,128)} %get-tuple-element.117), channel_id=1, source_target_pairs={{2,1},{4,3},{6,5},{10,9},{12,11},{14,13},{18,17},{20,19},{22,21},{... | collective-permute-start | bytes 23240 | tf_op jit(solution)/shard_map/ppermute | solution.py:80
  27.6 0.6 fusion.106
  28.4 10.3 %collective-permute-done.5 = f32[16,11,11]{2,1,0:T(8,128)} collective-permute-done((f32[16,11,11]{2,1,0:T(8,128)}, f32[16,11,11]{2,1,0:T(8,128)}, u32[]{:S(2)}, u32[]{:S(2)}) %collective-permute-start.5) | collective-permute-done | bytes 7776 | tf_op jit(solution)/shard_map/ppermute | solution.py:80
  38.6 3.3 %maximum_maximum_fusion = (f32[16,43,534]{2,1,0:T(8,128)S(1)}, f32[16,43,534]{2,1,0:T(8,128)S(1)}) fusion(f32[16,32,11]{2,1,0:T(8,128)S(1)} %collective-permute-done.4, f32[16,32,512]{2,1,0:T(8,128)S(1)} %copy-done, f32[16,32,11]{2,1,0:T(8,128)S(1)} %collective-permute-done.3, f32[16,11,11]{2,1,0:T(8,128)S(1)} %collective-permute-done.2, ...), kind=kLoop, calls=%fused_computation.7 | loop fusion | flops 3673920 | bytes 4784640 | tf_op jit(solution)/shard_map/concatenate | solution.py:86
  42.3 5.9 %fusion = f32[16,32,534]{2,1,0:T(8,128)S(1)} fusion(f32[16,43,534]{2,1,0:T(8,128)S(1)} %get-tuple-element.111, f32[16,43,534]{2,1,0:T(8,128)S(1)} %get-tuple-element.110, f32[16,32,11]{2,1,0:T(8,128)S(1)} %collective-permute-done.4, f32[16,32,512]{2,1,0:T(8,128)S(1)} %copy-done, f32[16,32,11]{2,1,0:T(8,128)S(1)} %collective-permute-done.3, ...), kind=kLoop, calls=%fused_computation.10 | loop fusion | flops 12850176 | bytes 26248640 | tf_op jit(solution)/shard_map/add | solution.py:125
  48.4 7.5 %select_bitcast_fusion = (f32[16,4,8,512]{3,2,1,0:T(8,128)S(1)}, f32[16,32,512]{2,1,0:T(8,128)S(1)}, pred[16,32,512]{2,1,0:T(8,128)(4,1)S(1)}) fusion(f32[16,32,534]{2,1,0:T(8,128)S(1)} %fusion, f32[16]{0:T(128)S(1)} %copy-done.6, f32[16]{0:T(128)S(1)} %copy-done.7, f32[16]{0:T(128)S(1)} %copy-done.8, f32[16]{0:T(128)S(1)} %copy-done.9, ...), kind=kLoop, calls=%fused_computation.103 | loop fusion | flops 12320768 | bytes 27526592 | tf_op jit(solution)/shard_map/reshape | solution.py:19
  56.1 3.4 %collective-permute-start.10 = (f32[16,8,512]{2,1,0:T(8,128)S(1)}, f32[16,8,512]{2,1,0:T(8,128)S(1)}, u32[]{:S(2)}, u32[]{:S(2)}) collective-permute-start(f32[16,8,512]{2,1,0:T(8,128)S(1)} %get-tuple-element.113), channel_id=1, source_target_pairs={{0,24},{8,16},{16,8},{24,0},{1,25},{9,17},{17,9},{25,1},{2,26},{10... | collective-permute-start | bytes 786440 | tf_op jit(solution)/shard_map/ppermute | solution.py:37
  59.5 0.4 collective-permute-start.8
  59.9 6.3 %collective-permute-done.10 = f32[16,8,512]{2,1,0:T(8,128)S(1)} collective-permute-done((f32[16,8,512]{2,1,0:T(8,128)S(1)}, f32[16,8,512]{2,1,0:T(8,128)S(1)}, u32[]{:S(2)}, u32[]{:S(2)}) %collective-permute-start.10) | collective-permute-done | bytes 262176 | tf_op jit(solution)/shard_map/ppermute | solution.py:37
  66.1 14.5 %collective-permute-done.9 = f32[16,8,512]{2,1,0:T(8,128)S(1)} collective-permute-done((f32[16,8,512]{2,1,0:T(8,128)S(1)}, f32[16,8,512]{2,1,0:T(8,128)S(1)}, u32[]{:S(2)}, u32[]{:S(2)}) %collective-permute-start.9) | collective-permute-done | bytes 262176 | tf_op jit(solution)/shard_map/ppermute | solution.py:37
  80.6 0.7 copy-done.3
  81.4 1.2 pad_maximum_fusion
  82.6 0.6 gather_fusion
  83.3 3.6 %while.13 = (s32[]{:T(128)}, f32[8,512]{1,0:T(8,128)S(1)}, f32[8,512]{1,0:T(8,128)S(1)}, f32[64,8,512]{2,1,0:T(8,128)S(1)}, f32[8,512]{1,0:T(8,128)S(1)}, /*index=5*/s32[]{:T(128)}, s32[]{:T(128)}) while((s32[]{:T(128)}, f32[8,512]{1,0:T(8,128)S(1)}, f32[8,512]{1,0:T(8,128)S(1)}, f32[64,8,512]{2,1,0:T(8,128)S(1)}, ...), condition=%wide.region_7.9_spmd.clone, body=%wide.region_5.8_spmd.clone.sunk | while | flops 1110019 | bytes 1302625 | solution.py:141
  87.0 0.2 fusion.22
  87.1 0.6 tile.2
  87.8 3.5 %all-to-all-start = ((f32[4,8,512]{2,1,0:T(8,128)}), f32[4,8,512]{2,1,0:T(8,128)S(1)}, u32[]{:S(2)}, u32[]{:S(2)}) async-start(f32[4,8,512]{2,1,0:T(8,128)} %tile.2), calls=%async_computation | async-start | bytes 131072 | tf_op jit(solution)/shard_map/all_to_all | solution.py:165
  91.2 5.0 %all-to-all-done = f32[4,8,512]{2,1,0:T(8,128)S(1)} async-done(((f32[4,8,512]{2,1,0:T(8,128)}), f32[4,8,512]{2,1,0:T(8,128)S(1)}, u32[]{:S(2)}, u32[]{:S(2)}) %all-to-all-start) | async-done | bytes 65568 | tf_op jit(solution)/shard_map/all_to_all | solution.py:165
  96.3 1.3 %collective-permute-start.15 = (f32[32,4]{1,0:T(8,128)S(1)}, f32[32,4]{1,0:T(8,128)S(1)}, u32[]{:S(2)}, u32[]{:S(2)}) collective-permute-start(f32[32,4]{1,0:T(8,128)S(1)} %get-tuple-element.149), channel_id=1, source_target_pairs={{1,0},{3,2},{5,4},{7,6},{9,8},{11,10},{13,12},{15,14},{17,16},{19,... | collective-permute-start | bytes 1544 | tf_op jit(solution)/shard_map/ppermute | solution.py:75
  97.7 1.3 %collective-permute-start.14 = (f32[32,4]{1,0:T(8,128)S(1)}, f32[32,4]{1,0:T(8,128)S(1)}, u32[]{:S(2)}, u32[]{:S(2)}) collective-permute-start(f32[32,4]{1,0:T(8,128)S(1)} %get-tuple-element.148), channel_id=1, source_target_pairs={{0,1},{2,3},{4,5},{6,7},{8,9},{10,11},{12,13},{14,15},{16,17},{18,... | collective-permute-start | bytes 1544 | tf_op jit(solution)/shard_map/ppermute | solution.py:75
  99.0 6.5 %collective-permute-start.13 = (f32[4,4]{1,0:T(4,128)S(1)}, f32[4,4]{1,0:T(4,128)S(1)}, u32[]{:S(2)}, u32[]{:S(2)}) collective-permute-start(f32[4,4]{1,0:T(4,128)S(1)} %get-tuple-element.145), channel_id=1, source_target_pairs={{1,2},{3,4},{5,6},{9,10},{11,12},{13,14},{17,18},{19,20},{21,22},{... | collective-permute-start | bytes 200 | tf_op jit(solution)/shard_map/ppermute | solution.py:80
  105.4 1.9 %collective-permute-start.12 = (f32[4,512]{1,0:T(4,128)S(1)}, f32[4,512]{1,0:T(4,128)S(1)}, u32[]{:S(2)}, u32[]{:S(2)}) collective-permute-start(f32[4,512]{1,0:T(4,128)S(1)} %get-tuple-element.146), channel_id=1, source_target_pairs={{0,2},{2,4},{4,6},{1,3},{3,5},{5,7},{8,10},{10,12},{12,14},{9,11},... | collective-permute-start | bytes 24584 | tf_op jit(solution)/shard_map/ppermute | solution.py:78
  107.4 1.3 %collective-permute-start.11 = (f32[4,4]{1,0:T(4,128)S(1)}, f32[4,4]{1,0:T(4,128)S(1)}, u32[]{:S(2)}, u32[]{:S(2)}) collective-permute-start(f32[4,4]{1,0:T(4,128)S(1)} %get-tuple-element.142), channel_id=1, source_target_pairs={{0,3},{2,5},{4,7},{8,11},{10,13},{12,15},{16,19},{18,21},{20,23},{... | collective-permute-start | bytes 200 | tf_op jit(solution)/shard_map/ppermute | solution.py:80
  108.7 4.3 %collective-permute-start.18 = (f32[4,4]{1,0:T(4,128)S(1)}, f32[4,4]{1,0:T(4,128)S(1)}, u32[]{:S(2)}, u32[]{:S(2)}) collective-permute-start(f32[4,4]{1,0:T(4,128)S(1)} %get-tuple-element.143), channel_id=1, source_target_pairs={{3,0},{5,2},{7,4},{11,8},{13,10},{15,12},{19,16},{21,18},{23,20},{... | collective-permute-start | bytes 200 | tf_op jit(solution)/shard_map/ppermute | solution.py:80
  112.9 1.9 %collective-permute-start.17 = (f32[4,512]{1,0:T(4,128)S(1)}, f32[4,512]{1,0:T(4,128)S(1)}, u32[]{:S(2)}, u32[]{:S(2)}) collective-permute-start(f32[4,512]{1,0:T(4,128)S(1)} %get-tuple-element.147), channel_id=1, source_target_pairs={{2,0},{4,2},{6,4},{3,1},{5,3},{7,5},{10,8},{12,10},{14,12},{11,9},... | collective-permute-start | bytes 24584 | tf_op jit(solution)/shard_map/ppermute | solution.py:78
  115.0 1.5 %collective-permute-start.16 = (f32[4,4]{1,0:T(4,128)S(1)}, f32[4,4]{1,0:T(4,128)S(1)}, u32[]{:S(2)}, u32[]{:S(2)}) collective-permute-start(f32[4,4]{1,0:T(4,128)S(1)} %get-tuple-element.144), channel_id=1, source_target_pairs={{2,1},{4,3},{6,5},{10,9},{12,11},{14,13},{18,17},{20,19},{22,21},{... | collective-permute-start | bytes 200 | tf_op jit(solution)/shard_map/ppermute | solution.py:80
  116.5 4.3 %collective-permute-done.16 = f32[4,4]{1,0:T(4,128)S(1)} collective-permute-done((f32[4,4]{1,0:T(4,128)S(1)}, f32[4,4]{1,0:T(4,128)S(1)}, u32[]{:S(2)}, u32[]{:S(2)}) %collective-permute-start.16) | collective-permute-done | bytes 96 | tf_op jit(solution)/shard_map/ppermute | solution.py:80
  121.0 0.6 multiply_add_fusion
  121.6 1.3 %fusion.45 = f32[8,32,512]{2,1,0:T(8,128)S(1)} fusion(f32[8,32,520]{2,1,0:T(8,128)S(1)} %multiply_add_fusion, f32[8]{0:T(128)S(1)} %get-tuple-element.151, f32[8]{0:T(128)S(1)} %get-tuple-element.152, f32[8]{0:T(128)S(1)} %get-tuple-element.153, f32[8]{0:T(128)S(1)} %get-tuple-element.154, f32[8]{0:T(128)S(1)} %get-tuple-element.155, ...), kind=kLoop, calls=%fused_computation.106 | loop fusion | flops 2228224 | bytes 5243168 | tf_op jit(solution)/shard_map/add | solution.py:180
  122.9 1.8 %subtract_select_fusion = f32[16,32,512]{2,1,0:T(8,128)} fusion(pred[16,32,512]{2,1,0:T(8,128)(4,1)S(1)} %get-tuple-element.109, f32[16,32,512]{2,1,0:T(8,128)S(1)} %get-tuple-element.108, f32[32,512]{1,0:T(8,128)S(1)} %get-tuple-element.125, f32[16]{0:T(128)S(1)} %get-tuple-element.160, f32[32,512]{1,0:T(8,128)S(1)} %get-tuple-element.126, ...), kind=kLoop, calls=%fused_computation.101 | loop fusion | flops 4456448 | bytes 2884096 | tf_op jit(solution)/shard_map/jit(_where)/select_n | solution.py:188
  124.7 0.6 copy.19
  (220 shorter events, 4.5 us)
Async XLA Ops:
  2.6 15.8 %copy-start.45 = (s32[16,2]{0,1:T(2,128)S(1)}, s32[16,2]{0,1:T(2,128)}, u32[]{:S(2)}) copy-start(s32[16,2]{0,1:T(2,128)} %param.11) | copy-start | bytes 388
  2.6 15.8 %copy-start.46 = (s32[16,2]{0,1:T(2,128)S(1)}, s32[16,2]{0,1:T(2,128)}, u32[]{:S(2)}) copy-start(s32[16,2]{0,1:T(2,128)} %param.10) | copy-start | bytes 388
  2.6 20.5 %collective-permute-start.2 = (f32[16,11,11]{2,1,0:T(8,128)S(1)}, f32[16,11,11]{2,1,0:T(8,128)S(1)}, u32[]{:S(2)}, u32[]{:S(2)}) collective-permute-start(f32[16,11,11]{2,1,0:T(8,128)S(1)} %get-tuple-element.118), channel_id=1, source_target_pairs={{1,2},{3,4},{5,6},{9,10},{11,12},{13,14},{17,18},{19,20},{21,22},{... | collective-permute-start | bytes 23240 | tf_op jit(solution)/shard_map/ppermute | solution.py:80
  7.4 13.0 %copy-start.47 = (s32[16]{0:T(128)S(1)}, s32[16]{0:T(128)}, u32[]{:S(2)}) copy-start(s32[16]{0:T(128)} %param.12) | copy-start | bytes 196
  7.4 31.3 %collective-permute-start.1 = (f32[16,11,512]{2,1,0:T(8,128)}, f32[16,11,512]{2,1,0:T(8,128)S(1)}, u32[]{:S(2)}, u32[]{:S(2)}) collective-permute-start(f32[16,11,512]{2,1,0:T(8,128)} %get-tuple-element.120), channel_id=1, source_target_pairs={{0,2},{2,4},{4,6},{1,3},{3,5},{5,7},{8,10},{10,12},{12,14},{9,11},... | collective-permute-start | bytes 1081352 | tf_op jit(solution)/shard_map/ppermute | solution.py:78
  9.4 15.0 %collective-permute-start = (f32[16,11,11]{2,1,0:T(8,128)S(1)}, f32[16,11,11]{2,1,0:T(8,128)S(1)}, u32[]{:S(2)}, u32[]{:S(2)}) collective-permute-start(f32[16,11,11]{2,1,0:T(8,128)S(1)} %get-tuple-element.116), channel_id=1, source_target_pairs={{0,3},{2,5},{4,7},{8,11},{10,13},{12,15},{16,19},{18,21},{20,23},{... | collective-permute-start | bytes 23240 | tf_op jit(solution)/shard_map/ppermute | solution.py:80
  10.7 15.6 %collective-permute-start.7 = (f32[16,11,11]{2,1,0:T(8,128)}, f32[16,11,11]{2,1,0:T(8,128)}, u32[]{:S(2)}, u32[]{:S(2)}) collective-permute-start(f32[16,11,11]{2,1,0:T(8,128)} %get-tuple-element.119), channel_id=1, source_target_pairs={{3,0},{5,2},{7,4},{11,8},{13,10},{15,12},{19,16},{21,18},{23,20},{... | collective-permute-start | bytes 23240 | tf_op jit(solution)/shard_map/ppermute | solution.py:80
  15.6 23.0 %collective-permute-start.6 = (f32[16,11,512]{2,1,0:T(8,128)S(1)}, f32[16,11,512]{2,1,0:T(8,128)S(1)}, u32[]{:S(2)}, u32[]{:S(2)}) collective-permute-start(f32[16,11,512]{2,1,0:T(8,128)S(1)} %get-tuple-element.121), channel_id=1, source_target_pairs={{2,0},{4,2},{6,4},{3,1},{5,3},{7,5},{10,8},{12,10},{14,12},{11,9},... | collective-permute-start | bytes 1081352 | tf_op jit(solution)/shard_map/ppermute | solution.py:78
  23.1 15.5 %collective-permute-start.4 = (f32[16,32,11]{2,1,0:T(8,128)}, f32[16,32,11]{2,1,0:T(8,128)S(1)}, u32[]{:S(2)}, u32[]{:S(2)}) collective-permute-start(f32[16,32,11]{2,1,0:T(8,128)} %get-tuple-element.123), channel_id=1, source_target_pairs={{1,0},{3,2},{5,4},{7,6},{9,8},{11,10},{13,12},{15,14},{17,16},{19,... | collective-permute-start | bytes 67592 | tf_op jit(solution)/shard_map/ppermute | solution.py:75
  25.0 13.6 %collective-permute-start.3 = (f32[16,32,11]{2,1,0:T(8,128)S(1)}, f32[16,32,11]{2,1,0:T(8,128)S(1)}, u32[]{:S(2)}, u32[]{:S(2)}) collective-permute-start(f32[16,32,11]{2,1,0:T(8,128)S(1)} %get-tuple-element.122), channel_id=1, source_target_pairs={{0,1},{2,3},{4,5},{6,7},{8,9},{10,11},{12,13},{14,15},{16,17},{18,... | collective-permute-start | bytes 67592 | tf_op jit(solution)/shard_map/ppermute | solution.py:75
  26.3 12.3 %collective-permute-start.5 = (f32[16,11,11]{2,1,0:T(8,128)}, f32[16,11,11]{2,1,0:T(8,128)}, u32[]{:S(2)}, u32[]{:S(2)}) collective-permute-start(f32[16,11,11]{2,1,0:T(8,128)} %get-tuple-element.117), channel_id=1, source_target_pairs={{2,1},{4,3},{6,5},{10,9},{12,11},{14,13},{18,17},{20,19},{22,21},{... | collective-permute-start | bytes 23240 | tf_op jit(solution)/shard_map/ppermute | solution.py:80
  28.2 13.7 %copy-start.28 = (f32[16]{0:T(128)S(1)}, f32[16]{0:T(128)}, u32[]{:S(2)}) copy-start(f32[16]{0:T(128)} %get-tuple-element.72) | copy-start | bytes 196
  28.2 13.7 %copy-start.29 = (f32[16]{0:T(128)S(1)}, f32[16]{0:T(128)}, u32[]{:S(2)}) copy-start(f32[16]{0:T(128)} %get-tuple-element.73) | copy-start | bytes 196
  28.2 13.7 %copy-start.30 = (f32[16]{0:T(128)S(1)}, f32[16]{0:T(128)}, u32[]{:S(2)}) copy-start(f32[16]{0:T(128)} %get-tuple-element.74) | copy-start | bytes 196
  28.2 13.7 %copy-start.31 = (f32[16]{0:T(128)S(1)}, f32[16]{0:T(128)}, u32[]{:S(2)}) copy-start(f32[16]{0:T(128)} %get-tuple-element.75) | copy-start | bytes 196
  28.2 13.7 %copy-start.32 = (f32[16]{0:T(128)S(1)}, f32[16]{0:T(128)}, u32[]{:S(2)}) copy-start(f32[16]{0:T(128)} %get-tuple-element.76) | copy-start | bytes 196
  28.2 13.7 %copy-start.33 = (f32[16]{0:T(128)S(1)}, f32[16]{0:T(128)}, u32[]{:S(2)}) copy-start(f32[16]{0:T(128)} %get-tuple-element.77) | copy-start | bytes 196
  28.2 13.7 %copy-start.34 = (f32[16]{0:T(128)S(1)}, f32[16]{0:T(128)}, u32[]{:S(2)}) copy-start(f32[16]{0:T(128)} %get-tuple-element.78) | copy-start | bytes 196
  28.3 13.7 %copy-start.35 = (f32[16]{0:T(128)S(1)}, f32[16]{0:T(128)}, u32[]{:S(2)}) copy-start(f32[16]{0:T(128)} %get-tuple-element.79) | copy-start | bytes 196
  28.3 13.7 %copy-start.36 = (f32[16]{0:T(128)S(1)}, f32[16]{0:T(128)}, u32[]{:S(2)}) copy-start(f32[16]{0:T(128)} %get-tuple-element.80) | copy-start | bytes 196
  28.3 13.7 %copy-start.37 = (f32[16]{0:T(128)S(1)}, f32[16]{0:T(128)}, u32[]{:S(2)}) copy-start(f32[16]{0:T(128)} %get-tuple-element.81) | copy-start | bytes 196
  28.3 13.7 %copy-start.38 = (f32[16]{0:T(128)S(1)}, f32[16]{0:T(128)}, u32[]{:S(2)}) copy-start(f32[16]{0:T(128)} %get-tuple-element.82) | copy-start | bytes 196
  28.3 13.7 %copy-start.39 = (f32[16]{0:T(128)S(1)}, f32[16]{0:T(128)}, u32[]{:S(2)}) copy-start(f32[16]{0:T(128)} %get-tuple-element.83) | copy-start | bytes 196
  28.3 13.7 %copy-start.40 = (f32[16]{0:T(128)S(1)}, f32[16]{0:T(128)}, u32[]{:S(2)}) copy-start(f32[16]{0:T(128)} %get-tuple-element.84) | copy-start | bytes 196
  28.3 13.7 %copy-start.41 = (f32[16]{0:T(128)S(1)}, f32[16]{0:T(128)}, u32[]{:S(2)}) copy-start(f32[16]{0:T(128)} %get-tuple-element.85) | copy-start | bytes 196
  28.3 13.7 %copy-start.42 = (f32[16]{0:T(128)S(1)}, f32[16]{0:T(128)}, u32[]{:S(2)}) copy-start(f32[16]{0:T(128)} %get-tuple-element.86) | copy-start | bytes 196
  28.3 13.7 %copy-start.43 = (f32[16]{0:T(128)S(1)}, f32[16]{0:T(128)}, u32[]{:S(2)}) copy-start(f32[16]{0:T(128)} %get-tuple-element.87) | copy-start | bytes 196
  28.3 13.7 %copy-start.44 = (f32[16]{0:T(128)S(1)}, f32[16]{0:T(128)}, u32[]{:S(2)}) copy-start(f32[16]{0:T(128)} %get-tuple-element.88) | copy-start | bytes 196
  42.1 6.1 %copy-start.1 = (s32[16,32,512]{2,1,0:T(8,128)S(1)}, s32[16,32,512]{2,1,0:T(8,128)}, u32[]{:S(2)}) copy-start(s32[16,32,512]{2,1,0:T(8,128)} %param.9) | copy-start | bytes 3145732
  42.1 6.1 %copy-start.6 = (f32[16]{0:T(128)S(1)}, f32[16]{0:T(128)}, u32[]{:S(2)}) copy-start(f32[16]{0:T(128)} %get-tuple-element.50) | copy-start | bytes 196
  42.1 6.1 %copy-start.7 = (f32[16]{0:T(128)S(1)}, f32[16]{0:T(128)}, u32[]{:S(2)}) copy-start(f32[16]{0:T(128)} %get-tuple-element.51) | copy-start | bytes 196
  42.1 6.1 %copy-start.8 = (f32[16]{0:T(128)S(1)}, f32[16]{0:T(128)}, u32[]{:S(2)}) copy-start(f32[16]{0:T(128)} %get-tuple-element.52) | copy-start | bytes 196
  42.1 6.1 %copy-start.9 = (f32[16]{0:T(128)S(1)}, f32[16]{0:T(128)}, u32[]{:S(2)}) copy-start(f32[16]{0:T(128)} %get-tuple-element.53) | copy-start | bytes 196
  42.1 6.1 %copy-start.10 = (f32[16]{0:T(128)S(1)}, f32[16]{0:T(128)}, u32[]{:S(2)}) copy-start(f32[16]{0:T(128)} %get-tuple-element.54) | copy-start | bytes 196
  42.1 6.1 %copy-start.11 = (f32[16]{0:T(128)S(1)}, f32[16]{0:T(128)}, u32[]{:S(2)}) copy-start(f32[16]{0:T(128)} %get-tuple-element.55) | copy-start | bytes 196
  56.1 10.1 %collective-permute-start.10 = (f32[16,8,512]{2,1,0:T(8,128)S(1)}, f32[16,8,512]{2,1,0:T(8,128)S(1)}, u32[]{:S(2)}, u32[]{:S(2)}) collective-permute-start(f32[16,8,512]{2,1,0:T(8,128)S(1)} %get-tuple-element.113), channel_id=1, source_target_pairs={{0,24},{8,16},{16,8},{24,0},{1,25},{9,17},{17,9},{25,1},{2,26},{10... | collective-permute-start | bytes 786440 | tf_op jit(solution)/shard_map/ppermute | solution.py:37
  59.5 21.2 %collective-permute-start.9 = (f32[16,8,512]{2,1,0:T(8,128)S(1)}, f32[16,8,512]{2,1,0:T(8,128)S(1)}, u32[]{:S(2)}, u32[]{:S(2)}) collective-permute-start(f32[16,8,512]{2,1,0:T(8,128)S(1)} %get-tuple-element.114), channel_id=1, source_target_pairs={{0,16},{8,24},{16,0},{24,8},{1,17},{9,25},{17,1},{25,9},{2,18},{10... | collective-permute-start | bytes 786440 | tf_op jit(solution)/shard_map/ppermute | solution.py:37
  59.5 21.2 %collective-permute-start.8 = (f32[16,8,512]{2,1,0:T(8,128)S(1)}, f32[16,8,512]{2,1,0:T(8,128)S(1)}, u32[]{:S(2)}, u32[]{:S(2)}) collective-permute-start(f32[16,8,512]{2,1,0:T(8,128)S(1)} %get-tuple-element.115), channel_id=1, source_target_pairs={{0,8},{8,0},{16,24},{24,16},{1,9},{9,1},{17,25},{25,17},{2,10},{10... | collective-permute-start | bytes 786440 | tf_op jit(solution)/shard_map/ppermute | solution.py:37
  66.1 14.5 %copy-start.2 = (f32[16,8,512]{2,1,0:T(8,128)}, f32[16,8,512]{2,1,0:T(8,128)S(1)}, u32[]{:S(2)}) copy-start(f32[16,8,512]{2,1,0:T(8,128)S(1)} %collective-permute-done.10) | copy-start | bytes 786436
  87.8 8.5 %all-to-all-start = ((f32[4,8,512]{2,1,0:T(8,128)}), f32[4,8,512]{2,1,0:T(8,128)S(1)}, u32[]{:S(2)}, u32[]{:S(2)}) async-start(f32[4,8,512]{2,1,0:T(8,128)} %tile.2), calls=%async_computation | async-start | bytes 131072 | tf_op jit(solution)/shard_map/all_to_all | solution.py:165
  96.3 12.3 %collective-permute-start.15 = (f32[32,4]{1,0:T(8,128)S(1)}, f32[32,4]{1,0:T(8,128)S(1)}, u32[]{:S(2)}, u32[]{:S(2)}) collective-permute-start(f32[32,4]{1,0:T(8,128)S(1)} %get-tuple-element.149), channel_id=1, source_target_pairs={{1,0},{3,2},{5,4},{7,6},{9,8},{11,10},{13,12},{15,14},{17,16},{19,... | collective-permute-start | bytes 1544 | tf_op jit(solution)/shard_map/ppermute | solution.py:75
  97.7 15.3 %collective-permute-start.14 = (f32[32,4]{1,0:T(8,128)S(1)}, f32[32,4]{1,0:T(8,128)S(1)}, u32[]{:S(2)}, u32[]{:S(2)}) collective-permute-start(f32[32,4]{1,0:T(8,128)S(1)} %get-tuple-element.148), channel_id=1, source_target_pairs={{0,1},{2,3},{4,5},{6,7},{8,9},{10,11},{12,13},{14,15},{16,17},{18,... | collective-permute-start | bytes 1544 | tf_op jit(solution)/shard_map/ppermute | solution.py:75
  99.0 16.0 %collective-permute-start.13 = (f32[4,4]{1,0:T(4,128)S(1)}, f32[4,4]{1,0:T(4,128)S(1)}, u32[]{:S(2)}, u32[]{:S(2)}) collective-permute-start(f32[4,4]{1,0:T(4,128)S(1)} %get-tuple-element.145), channel_id=1, source_target_pairs={{1,2},{3,4},{5,6},{9,10},{11,12},{13,14},{17,18},{19,20},{21,22},{... | collective-permute-start | bytes 200 | tf_op jit(solution)/shard_map/ppermute | solution.py:80
  105.4 15.4 %collective-permute-start.12 = (f32[4,512]{1,0:T(4,128)S(1)}, f32[4,512]{1,0:T(4,128)S(1)}, u32[]{:S(2)}, u32[]{:S(2)}) collective-permute-start(f32[4,512]{1,0:T(4,128)S(1)} %get-tuple-element.146), channel_id=1, source_target_pairs={{0,2},{2,4},{4,6},{1,3},{3,5},{5,7},{8,10},{10,12},{12,14},{9,11},... | collective-permute-start | bytes 24584 | tf_op jit(solution)/shard_map/ppermute | solution.py:78
  107.4 9.1 %collective-permute-start.11 = (f32[4,4]{1,0:T(4,128)S(1)}, f32[4,4]{1,0:T(4,128)S(1)}, u32[]{:S(2)}, u32[]{:S(2)}) collective-permute-start(f32[4,4]{1,0:T(4,128)S(1)} %get-tuple-element.142), channel_id=1, source_target_pairs={{0,3},{2,5},{4,7},{8,11},{10,13},{12,15},{16,19},{18,21},{20,23},{... | collective-permute-start | bytes 200 | tf_op jit(solution)/shard_map/ppermute | solution.py:80
  108.7 7.8 %collective-permute-start.18 = (f32[4,4]{1,0:T(4,128)S(1)}, f32[4,4]{1,0:T(4,128)S(1)}, u32[]{:S(2)}, u32[]{:S(2)}) collective-permute-start(f32[4,4]{1,0:T(4,128)S(1)} %get-tuple-element.143), channel_id=1, source_target_pairs={{3,0},{5,2},{7,4},{11,8},{13,10},{15,12},{19,16},{21,18},{23,20},{... | collective-permute-start | bytes 200 | tf_op jit(solution)/shard_map/ppermute | solution.py:80
  112.9 7.8 %collective-permute-start.17 = (f32[4,512]{1,0:T(4,128)S(1)}, f32[4,512]{1,0:T(4,128)S(1)}, u32[]{:S(2)}, u32[]{:S(2)}) collective-permute-start(f32[4,512]{1,0:T(4,128)S(1)} %get-tuple-element.147), channel_id=1, source_target_pairs={{2,0},{4,2},{6,4},{3,1},{5,3},{7,5},{10,8},{12,10},{14,12},{11,9},... | collective-permute-start | bytes 24584 | tf_op jit(solution)/shard_map/ppermute | solution.py:78
  115.0 5.8 %collective-permute-start.16 = (f32[4,4]{1,0:T(4,128)S(1)}, f32[4,4]{1,0:T(4,128)S(1)}, u32[]{:S(2)}, u32[]{:S(2)}) collective-permute-start(f32[4,4]{1,0:T(4,128)S(1)} %get-tuple-element.144), channel_id=1, source_target_pairs={{2,1},{4,3},{6,5},{10,9},{12,11},{14,13},{18,17},{20,19},{22,21},{... | collective-permute-start | bytes 200 | tf_op jit(solution)/shard_map/ppermute | solution.py:80
  (21 other events, 109.3 us)
